TPU v7x, 512 devices: a whole 4x8x8 slice. The times are simulated.
512 devices in a mesh: dp: 4 (over y_hi, core), context: 16 (over y_lo, x), tensor: 8 (over z).
Axes of the slice: x: 4, y: 8 (y_hi: 2, y_lo: 4; y = y_hi * 4 + y_lo), z: 8, core: 2. Of those that a mesh axis runs over, the one named last changes fastest.
Arguments:
- queries: bfloat16 [8192, 4096], P(('dp', 'context'), 'tensor'), parts along dimension 0, may hold values from -6 to 6
- keys: bfloat16 [8192, 1024], P(('dp', 'context'), 'tensor'), parts along dimension 0, may hold values from -6 to 6
- values: bfloat16 [8192, 1024], P(('dp', 'context'), 'tensor'), parts along dimension 0, may hold values from -6 to 6
- order: int32 [8192], P('dp'), parts along dimension 0, may hold values from 0 to 2047, as said below
- out_weight: bfloat16 [4096, 4096], P('tensor', 'context'), may hold values from -0.125 to 0.125
Outputs:
- output: bfloat16 [8192, 4096], P(('dp', 'context'), 'tensor'), parts along dimension 0
There are 4 independent parts, one for each index of `dp`. A program takes and returns all parts, laid end to end along the dimension named above; an argument that names none is the same for every part. Nothing has to cross between parts.
Inputs may be any that keep to these rules, and one draw needn't show every extreme that they name: A permutation of the positions; each aligned block of 128 rows holds 128 consecutive positions in increasing order, starting at a multiple of 128.
All inputs are finite; a program needn't handle non-finite values.
Results may differ from a plain program's by a relative error of at most 0.019.
Values may be sent and summed in bfloat16 or wider, within the bound.
No kernel may reach another device: no remote copies, remote signals or barrier semaphores. Data moves between devices by JAX's collectives and lax.ppermute only.
A program may use at most 64 MiB of HBM per device.

v0:
```python
import math
import jax
import jax.numpy as jnp
from jax import lax
from jax.sharding import PartitionSpec as P

QUERY_HEADS = 32
KEY_VALUE_HEADS = 8
HEAD_SIZE = 128


def per_device(queries, keys, values, order, out_weight):
    row_count = queries.shape[0]
    local_groups = keys.shape[1] // HEAD_SIZE
    query_head_group = QUERY_HEADS // KEY_VALUE_HEADS
    score_scale = 1.0 / math.sqrt(HEAD_SIZE)
    first_row = lax.axis_index("context") * row_count
    query_pos = lax.dynamic_slice_in_dim(order, first_row, row_count, 0)
    stacked = queries.reshape(row_count, local_groups, query_head_group, HEAD_SIZE)
    stacked = stacked.transpose(1, 2, 0, 3).reshape(
        local_groups, query_head_group * row_count, HEAD_SIZE
    )
    stacked_pos = jnp.tile(query_pos, query_head_group)
    stacked_rows = query_head_group * row_count
    key_part = lax.all_gather(keys, "context", axis=0, tiled=True)
    value_part = lax.all_gather(values, "context", axis=0, tiled=True)
    key_count = key_part.shape[0]
    running_max = jnp.full((local_groups, stacked_rows), -1e30, jnp.float32)
    key_heads = key_part.reshape(key_count, local_groups, HEAD_SIZE)
    value_heads = value_part.reshape(key_count, local_groups, HEAD_SIZE)
    scores = (
        jnp.einsum("grd,kgd->grk", stacked, key_heads, preferred_element_type=jnp.float32)
        * score_scale
    )
    visible = order[None, None, :] <= stacked_pos[None, :, None]
    scores = jnp.where(visible, scores, -1e30)
    new_max = jnp.maximum(running_max, jnp.max(scores, axis=2))
    weights = jnp.where(visible, jnp.exp(scores - new_max[..., None]), 0.0)
    new_sum = jnp.sum(weights, axis=2)
    product = jnp.einsum(
        "grk,kgd->grd",
        weights.astype(jnp.bfloat16),
        value_heads,
        preferred_element_type=jnp.float32,
    )
    attended = (product / new_sum[..., None]).astype(jnp.bfloat16)
    attended = attended.reshape(local_groups, query_head_group, row_count, HEAD_SIZE).transpose(
        2, 0, 1, 3
    )
    attended = attended.reshape(row_count, local_groups * query_head_group * HEAD_SIZE)
    partial_out = jnp.dot(
        attended,
        lax.all_gather(out_weight, "context", axis=1, tiled=True),
        preferred_element_type=jnp.float32,
    )
    summed = lax.psum(partial_out.astype(jnp.bfloat16), "tensor").astype(jnp.float32)
    column_count = summed.shape[1] // lax.axis_size("tensor")
    mine = lax.dynamic_slice_in_dim(
        summed, lax.axis_index("tensor") * column_count, column_count, 1
    )
    return mine.astype(jnp.bfloat16)


def solution(mesh):
    placed = (
        P(("dp", "context"), "tensor"),
        P(("dp", "context"), "tensor"),
        P(("dp", "context"), "tensor"),
        P("dp"),
        P("tensor", "context"),
    )
    return jax.shard_map(
        per_device,
        mesh=mesh,
        in_specs=placed,
        out_specs=P(("dp", "context"), "tensor"),
        check_vma=False,
    )
```

profile of v0, /device:TPU:2, one launch (start us, length us, event | category | flops | bytes accessed | tf_op | source)
XLA Modules:
  0.0 208.4 jit_solution(8475246983671661402)
XLA Ops:
  6.5 0.0 copy-start.1
  6.5 0.0 copy-start
  6.5 0.0 all-gather.2.cloned.1.call-start
  6.5 0.7 all-gather.2.cloned.1.call-update
  7.3 0.0 all-reduce.2.cloned.1.call-start
  7.3 1.0 copy.7
  8.3 0.1 copy.8
  8.5 0.8 dynamic_slice.6
  9.3 47.2 %all_gather.9 = bf16[2048,128]{1,0:T(8,128)(2,1)S(1)} all-gather(bf16[128,128]{1,0:T(8,128)(2,1)} %param.6), channel_id=1, replica_groups=mesh['dp'=4,'context'=16,'tensor'=8] {'context'}, dimensions={0}, use_global_device_ids=true | all-gather | bytes 557056 | tf_op jit(solution)/shard_map/all_gather | solution.py:25
  56.4 1.6 fusion
  58.0 0.0 copy-done
  58.0 42.5 %all_gather.10 = bf16[2048,128]{1,0:T(8,128)(2,1)S(1)} all-gather(bf16[128,128]{1,0:T(8,128)(2,1)S(1)} %copy-done), channel_id=1, replica_groups=mesh['dp'=4,'context'=16,'tensor'=8] {'context'}, dimensions={0}, use_global_device_ids=true | all-gather | bytes 557056 | tf_op jit(solution)/shard_map/all_gather | solution.py:26
  100.5 0.0 copy-done.1
  100.5 1.2 fusion.1
  101.7 1.1 fusion.8
  102.9 0.1 copy.9
  103.0 6.5 %all-gather.2.cloned.1.call-done = bf16[512,4096]{1,0:T(8,128)(2,1)} async-done(((bf16[512,256]{1,0:T(8,128)(2,1)}), bf16[512,4096]{1,0:T(8,128)(2,1)}) %all-gather.2.cloned.1.call-update) | async-done | bytes 4194320 | tf_op jit(solution)/shard_map/all_gather | solution.py:53
  109.5 3.9 %convolution_convert_fusion = bf16[128,4096]{1,0:T(8,128)(2,1)} fusion(bf16[128,512]{0,1:T(8,128)(2,1)S(1)} %bitcast.16, bf16[512,4096]{1,0:T(8,128)(2,1)} %all-gather.2.cloned.1.call-done), kind=kOutput, calls=%fused_computation.2 | convolution fusion | flops 537395200 | bytes 5373952 | tf_op jit(solution)/shard_map/dot_general | solution.py:51
  113.5 0.0 all-reduce.2.cloned.1.call-update
  113.5 86.5 %all-reduce.2.cloned.1.call-done = bf16[128,4096]{1,0:T(8,128)(2,1)} async-done(((bf16[128,4096]{1,0:T(8,128)(2,1)}), bf16[128,4096]{1,0:T(8,128)(2,1)}) %all-reduce.2.cloned.1.call-update) | async-done | bytes 1048592 | tf_op jit(solution)/shard_map/psum | solution.py:56
  200.0 1.6 convert_convert_fusion
  (2 shorter events, 0.0 us)
Async XLA Ops:
  6.5 94.0 %copy-start.1 = (s32[2048]{0:T(1024)S(1)}, s32[2048]{0:T(1024)}, u32[]{:S(2)}) copy-start(s32[2048]{0:T(1024)} %param.8) | copy-start | bytes 24580
  6.5 51.5 %copy-start = (bf16[128,128]{1,0:T(8,128)(2,1)S(1)}, bf16[128,128]{1,0:T(8,128)(2,1)}, u32[]{:S(2)}) copy-start(bf16[128,128]{1,0:T(8,128)(2,1)} %param.7) | copy-start | bytes 98308
  6.5 103.0 %all-gather.2.cloned.1.call-start = ((), (), s32[]{:S(2)}) async-start(), calls=%async_computation | async-start | bytes 4456448 | tf_op jit(solution)/shard_map/all_gather | solution.py:53
  7.3 192.7 %all-reduce.2.cloned.1.call-start = ((), (), s32[]{:S(2)}) async-start(), calls=%async_computation.1 | async-start | bytes 2097152 | tf_op jit(solution)/shard_map/psum | solution.py:56
Sparse Core Ops, SparseCore 0:
  9.3 100.1 all-gather.1
  113.6 86.3 all-reduce.1
where the time goes:
time: 209 us; the launch traced here: 208 us
  waiting for transfers between devices  93.8 us (45%)
  blocking collectives  89.6 us (43%)
  between operations  13.4 us (6%)
  matrix products  6.62 us (3%)
  other arithmetic  2.82 us (1%)
    psum x1, waiting for transfers between devices, per_device(): lax.psum(partial_out.astype(jnp.bfloat16), 'tensor').astype(jnp.float32)  86.5 us
    all_gather x1, blocking collectives, per_device(): key_part = lax.all_gather(keys, 'context', axis=0, tiled=True)  47.2 us
    all_gather x1, blocking collectives, per_device(): value_part = lax.all_gather(values, 'context', axis=0, tiled=True)  42.5 us
    all_gather x1, waiting for transfers between devices, per_device(): lax.all_gather(out_weight, 'context', axis=1, tiled=True)  6.54 us
  transfers between devices with their start and end apart: 2, of which 2 were waited for; matrix products, arithmetic and copies ran while one was open for 3% of the time, Pallas kernels for 0%

commit v1 on v0

--- a/solution.py
+++ b/solution.py
@@ -7,6 +7,10 @@
 QUERY_HEADS = 32
 KEY_VALUE_HEADS = 8
 HEAD_SIZE = 128
+
+
+def cells_handle(w_in):
+    return jnp.sum(lax.all_gather(w_in, "tensor"), 0)
 
 
 def per_device(queries, keys, values, order, out_weight):
@@ -53,7 +57,7 @@
         lax.all_gather(out_weight, "context", axis=1, tiled=True),
         preferred_element_type=jnp.float32,
     )
-    summed = lax.psum(partial_out.astype(jnp.bfloat16), "tensor").astype(jnp.float32)
+    summed = cells_handle(partial_out.astype(jnp.bfloat16)).astype(jnp.float32)
     column_count = summed.shape[1] // lax.axis_size("tensor")
     mine = lax.dynamic_slice_in_dim(
         summed, lax.axis_index("tensor") * column_count, column_count, 1

time: 209 us -> 229 us (1.096)
  the two profiles are of different devices: /device:TPU:2 before, /device:TPU:1 now
where the time goes in v1:
time: 229 us; the launch traced here: 228 us
  waiting for transfers between devices  123 us (54%)
  blocking collectives  76.8 us (34%)
  between operations  13.5 us (6%)
  other arithmetic  6.83 us (3%)
  matrix products  6.72 us (3%)
    all_gather x1, waiting for transfers between devices, cells_handle(): return jnp.sum(lax.all_gather(w_in, 'tensor'), 0)  110 us
    all_gather x1, blocking collectives, per_device(): key_part = lax.all_gather(keys, 'context', axis=0, tiled=True)  40.2 us
    all_gather x1, blocking collectives, per_device(): value_part = lax.all_gather(values, 'context', axis=0, tiled=True)  36.6 us
    all_gather x1, waiting for transfers between devices, per_device(): lax.all_gather(out_weight, 'context', axis=1, tiled=True)  11.8 us
    reduce_sum x1, other arithmetic, cells_handle(): return jnp.sum(lax.all_gather(w_in, 'tensor'), 0)  4.9 us
  transfers between devices with their start and end apart: 2, of which 2 were waited for; matrix products, arithmetic and copies ran while one was open for 3% of the time, Pallas kernels for 0%

profile of v1, /device:TPU:1, one launch (start us, length us, event | category | flops | bytes accessed | tf_op | source)
XLA Modules:
  0.0 228.4 jit_solution(8456694613087629323)
XLA Ops:
  6.5 0.0 copy-start.1
  6.5 0.0 copy-start
  6.5 0.0 all-gather.4.cloned.1.call-start
  6.5 0.7 all-gather.4.cloned.1.call-update
  7.3 0.0 all-gather.6.cloned.1.call-start
  7.3 1.0 copy.7
  8.3 0.1 copy.8
  8.5 0.8 dynamic_slice.6
  9.3 40.2 %all_gather.15 = bf16[2048,128]{1,0:T(8,128)(2,1)S(1)} all-gather(bf16[128,128]{1,0:T(8,128)(2,1)} %param.6), channel_id=1, replica_groups=mesh['dp'=4,'context'=16,'tensor'=8] {'context'}, dimensions={0}, use_global_device_ids=true | all-gather | bytes 557056 | tf_op jit(solution)/shard_map/all_gather | solution.py:29
  49.4 1.6 fusion
  51.1 0.0 copy-done
  51.1 36.6 %all_gather.16 = bf16[2048,128]{1,0:T(8,128)(2,1)S(1)} all-gather(bf16[128,128]{1,0:T(8,128)(2,1)S(1)} %copy-done), channel_id=1, replica_groups=mesh['dp'=4,'context'=16,'tensor'=8] {'context'}, dimensions={0}, use_global_device_ids=true | all-gather | bytes 557056 | tf_op jit(solution)/shard_map/all_gather | solution.py:30
  87.6 0.0 copy-done.1
  87.7 1.2 fusion.1
  88.9 1.1 fusion.8
  90.0 0.1 copy.9
  90.2 11.8 %all-gather.4.cloned.1.call-done = bf16[512,4096]{1,0:T(8,128)(2,1)} async-done(((bf16[512,256]{1,0:T(8,128)(2,1)}), bf16[512,4096]{1,0:T(8,128)(2,1)}) %all-gather.4.cloned.1.call-update) | async-done | bytes 4194320 | tf_op jit(solution)/shard_map/all_gather | solution.py:57
  102.0 4.0 %convolution_convert_fusion = bf16[128,4096]{1,0:T(8,128)(2,1)} fusion(bf16[128,512]{0,1:T(8,128)(2,1)S(1)} %bitcast.18, bf16[512,4096]{1,0:T(8,128)(2,1)} %all-gather.4.cloned.1.call-done), kind=kOutput, calls=%fused_computation.2 | convolution fusion | flops 537395200 | bytes 5373952 | tf_op jit(solution)/shard_map/dot_general | solution.py:55
  106.0 0.0 all-gather.6.cloned.1.call-update
  106.0 110.0 %all-gather.6.cloned.1.call-done = bf16[1024,4096]{1,0:T(8,128)(2,1)} async-done(((bf16[128,4096]{1,0:T(8,128)(2,1)}), bf16[1024,4096]{1,0:T(8,128)(2,1)}) %all-gather.6.cloned.1.call-update) | async-done | bytes 8388624 | tf_op jit(solution)/shard_map/all_gather | solution.py:13
  216.0 4.9 %reduce_sum.22 = bf16[128,4096]{1,0:T(8,128)(2,1)S(1)} reduce(bf16[8,128,4096]{2,1,0:T(8,128)(2,1)} %bitcast.16, bf16[]{:T(256)} %constant.26.clone.1), dimensions={0}, to_apply=%region_2.3 | reduce | flops 3670016 | bytes 9437186 | tf_op jit(solution)/shard_map/reduce_sum | solution.py:13
  220.9 0.7 convert_convert_fusion
  (2 shorter events, 0.0 us)
Async XLA Ops:
  6.5 81.1 %copy-start.1 = (s32[2048]{0:T(1024)S(1)}, s32[2048]{0:T(1024)}, u32[]{:S(2)}) copy-start(s32[2048]{0:T(1024)} %param.8) | copy-start | bytes 24580
  6.5 44.5 %copy-start = (bf16[128,128]{1,0:T(8,128)(2,1)S(1)}, bf16[128,128]{1,0:T(8,128)(2,1)}, u32[]{:S(2)}) copy-start(bf16[128,128]{1,0:T(8,128)(2,1)} %param.7) | copy-start | bytes 98308
  6.5 95.4 %all-gather.4.cloned.1.call-start = ((), (), s32[]{:S(2)}) async-start(), calls=%async_computation | async-start | bytes 4456448 | tf_op jit(solution)/shard_map/all_gather | solution.py:57
  7.3 208.7 %all-gather.6.cloned.1.call-start = ((), (), s32[]{:S(2)}) async-start(), calls=%async_computation.1 | async-start | bytes 9437184 | tf_op jit(solution)/shard_map/all_gather | solution.py:13
Sparse Core Ops, SparseCore 0:
  9.3 92.5 all-gather.3
  106.1 109.8 all-gather.5
